TPU v7x, 256 devices: a whole 4x4x8 slice. The times are simulated.
256 devices in a mesh: dp: 8 (over x, z_hi), tensor: 32 (over y, z_lo, core).
Axes of the slice: x: 4, y: 4, z: 8 (z_hi: 2, z_lo: 4; z = z_hi * 4 + z_lo), core: 2. Of those that a mesh axis runs over, the one named last changes fastest.
Arguments:
- tokens: bfloat16 [8, 4096, 1280], P('dp', 'tensor'), may hold values from -6 to 6
- segment_ids: int32 [8, 4096], P('dp', 'tensor'), may hold values from 0 to 3, never falling along the last dimension, each value on 1 to 2048 neighbouring positions
- pack_of_group: int32 [32], replicated, may hold values from 0 to 31, each once
- w_qkv: bfloat16 [1280, 1920], replicated, may hold values from -0.11320094 to 0.11320094
- qk_gain: float32 [640], replicated, may hold values from 0.5 to 7
- w_out: bfloat16 [640, 1280], replicated, may hold values from -0.25 to 0.25
- alpha_attn: float32 [1280], replicated, may hold values from 0.05 to 0.6
- w_up: bfloat16 [1280, 5120], P(None, 'dp'), may hold values from -0.15625 to 0.15625
- w_gate: bfloat16 [1280, 5120], P(None, 'dp'), may hold values from -0.15625 to 0.15625
- up_gain: float32 [5120], P('dp'), may hold values from 0.5 to 2
- gate_gain: float32 [5120], P('dp'), may hold values from 0.5 to 2
- w_down: bfloat16 [5120, 1280], P('dp'), may hold values from -0.078125 to 0.078125
- alpha_mlp: float32 [1280], replicated, may hold values from 0.05 to 0.6
- w_vocab: bfloat16 [1280, 32000], P(None, ('dp', 'tensor')), may hold values from -0.15625 to 0.15625
- logit_gain: bfloat16 [32000], P(('dp', 'tensor')), may hold values from 1 to 10
Outputs:
- result_rows: bfloat16 [8, 4096, 1280], P('dp', 'tensor')
- request_norm: float32 [32], replicated
- max_logit: float32 [32], replicated
Inputs may be any that keep to these rules, and one draw needn't show every extreme that they name: `segment_ids`: within a pack the request numbers never fall, every request 0 to 3 has one or more tokens, and one request has exactly 2048 tokens.
All inputs are finite; a program needn't handle non-finite values.
Results may differ from a plain program's by a relative error of at most 0.013.
Values may be sent and summed in bfloat16 or wider, within the bound.
No kernel may reach another device: no remote copies, remote signals or barrier semaphores. Data moves between devices by JAX's collectives and lax.ppermute only.
A program may use at most 128 MiB of HBM per device.

v0:
```python
import math
import jax
import jax.numpy as jnp
from jax import lax
from jax.sharding import PartitionSpec as P

HEADS = 10
HD = 64
REQS = 4
EPSILON = 1e-06
NEGATIVE = -1e30


def normalize(values):
    return values * lax.rsqrt(jnp.mean(values * values, axis=-1, keepdims=True) + EPSILON)


def head_norm(values, qk_gain):
    reshaped = values.reshape(values.shape[0], HEADS, HD)
    return (normalize(reshaped) * qk_gain.reshape(HEADS, HD)).astype(jnp.bfloat16)


def local(
    tokens,
    segment_ids,
    pack_of_group,
    w_qkv,
    qk_gain,
    w_out,
    alpha_attn,
    w_up,
    w_gate,
    up_gain,
    gate_gain,
    w_down,
    alpha_mlp,
    w_vocab,
    logit_gain,
):
    row_count = tokens.shape[1]
    head_width = HEADS * HD
    segments = segment_ids[0]
    tensor_index = lax.axis_index("tensor")
    positions = tensor_index * row_count + jnp.arange(row_count, dtype=jnp.int32)
    request_numbers = jnp.arange(REQS, dtype=jnp.int32)
    start_rows = normalize(tokens[0].astype(jnp.float32)).astype(jnp.bfloat16)
    projected = jnp.dot(start_rows, w_qkv, preferred_element_type=jnp.float32)
    queries = head_norm(projected[:, :head_width], qk_gain)
    key_rows = head_norm(projected[:, head_width : 2 * head_width], qk_gain).reshape(
        row_count, head_width
    )
    value_rows = projected[:, 2 * head_width :].astype(jnp.bfloat16)
    score_scale = 1.0 / math.sqrt(HD)
    offset = jnp.int32(0)
    state_now = (
        jnp.full((HEADS, row_count), NEGATIVE, jnp.float32),
        jnp.zeros((HEADS, row_count), jnp.float32),
        jnp.zeros((HEADS, row_count, HD), jnp.float32),
    )
    key_all = lax.all_gather(key_rows, "tensor", axis=0, tiled=True)
    value_all = lax.all_gather(value_rows, "tensor", axis=0, tiled=True)
    seg_all = lax.all_gather(segments, "tensor", axis=0, tiled=True)
    tally = jnp.sum((seg_all[:, None] == request_numbers[None, :]).astype(jnp.int32), axis=0)
    total_keys = key_all.shape[0]
    step_size = math.gcd(total_keys, 512)
    for begin in range(0, total_keys, step_size):
        key_part = key_all[begin : begin + step_size]
        value_part = value_all[begin : begin + step_size]
        seg_part = seg_all[begin : begin + step_size]
        key_pos = offset + begin + jnp.arange(step_size, dtype=jnp.int32)
        update_running_max, update_weight_sum, update_weighted = state_now
        key_count = key_part.shape[0]
        key_heads = key_part.reshape(key_count, HEADS, HD)
        value_heads = value_part.reshape(key_count, HEADS, HD)
        scores = (
            jnp.einsum("qhd,khd->hqk", queries, key_heads, preferred_element_type=jnp.float32)
            * score_scale
        )
        allowed = (seg_part[None, :] == segments[:, None]) & (
            key_pos[None, :] <= positions[:, None]
        )
        new_max = jnp.maximum(
            update_running_max, jnp.max(jnp.where(allowed[None], scores, NEGATIVE), axis=2)
        )
        weights = jnp.where(allowed[None], jnp.exp(scores - new_max[:, :, None]), 0.0)
        factor = jnp.exp(update_running_max - new_max)
        update_weight_sum = update_weight_sum * factor + jnp.sum(weights, axis=2)
        update_weighted = update_weighted * factor[:, :, None] + jnp.einsum(
            "hqk,khd->hqd",
            weights.astype(jnp.bfloat16),
            value_heads,
            preferred_element_type=jnp.float32,
        )
        state_now = (new_max, update_weight_sum, update_weighted)
    folded, tally = (state_now, tally)
    running_max, weight_sum, weighted = folded
    attended = (
        (weighted / weight_sum[:, :, None])
        .transpose(1, 0, 2)
        .reshape(row_count, head_width)
        .astype(jnp.bfloat16)
    )
    attn_rows = normalize(jnp.dot(attended, w_out, preferred_element_type=jnp.float32))
    residual_in = start_rows.astype(jnp.float32)
    mid_rows = normalize(residual_in + alpha_attn * (attn_rows - residual_in)).astype(jnp.bfloat16)
    received = lax.all_gather(mid_rows, "dp", axis=0, tiled=True)
    up_proj = jnp.dot(received, w_up, preferred_element_type=jnp.float32) * up_gain
    gate_proj = jnp.dot(received, w_gate, preferred_element_type=jnp.float32) * gate_gain
    hidden = (up_proj * jax.nn.silu(gate_proj)).astype(jnp.bfloat16)
    mixed_sum = lax.psum_scatter(
        jnp.dot(hidden, w_down, preferred_element_type=jnp.float32).astype(jnp.bfloat16),
        "dp",
        scatter_dimension=0,
        tiled=True,
    ).astype(jnp.float32)
    mlp_rows = normalize(mixed_sum)
    residual_mid = mid_rows.astype(jnp.float32)
    result_rows = normalize(residual_mid + alpha_mlp * (mlp_rows - residual_mid)).astype(
        jnp.bfloat16
    )
    request_ends = jnp.cumsum(tally) - 1
    same_request = segments[:, None] == request_numbers[None, :]
    row_end = jnp.sum(jnp.where(same_request, request_ends[None, :], 0), axis=1)
    is_last = positions == row_end
    member = same_request.astype(jnp.float32)
    chosen = member * is_last[:, None].astype(jnp.float32)
    result_f32 = result_rows.astype(jnp.float32)
    row_sums = jnp.dot(member.T, result_f32, precision=lax.Precision.HIGHEST)
    last_rows = jnp.dot(chosen.T, result_f32, precision=lax.Precision.HIGHEST)
    counts = jnp.sum(member, axis=0)
    row_sums, last_rows, counts = (
        lax.psum(row_sums.astype(jnp.bfloat16), "tensor").astype(jnp.float32),
        lax.psum(last_rows.astype(jnp.bfloat16), "tensor").astype(jnp.float32),
        lax.psum(counts.astype(jnp.bfloat16), "tensor").astype(jnp.float32),
    )
    request_mean = row_sums / counts[:, None]
    group_norm = jnp.sqrt(jnp.mean(request_mean * request_mean, axis=1))
    slot_count = lax.axis_size("dp") * REQS
    every_last, every_norm = (
        lax.all_gather(last_rows, "dp", axis=0, tiled=True),
        lax.all_gather(group_norm, "dp", axis=0, tiled=True),
    )
    logits = jnp.dot(
        every_last.astype(jnp.bfloat16), w_vocab, preferred_element_type=jnp.float32
    ) * logit_gain.astype(jnp.float32)
    every_max = lax.pmax(jnp.max(logits, axis=1), ("dp", "tensor"))
    placement = (pack_of_group[:, None] == jnp.arange(slot_count, dtype=jnp.int32)[None, :]).astype(
        jnp.float32
    )
    request_norm = jnp.dot(every_norm, placement, precision=lax.Precision.HIGHEST)
    max_logit = jnp.dot(every_max, placement, precision=lax.Precision.HIGHEST)
    return (result_rows[None], request_norm, max_logit)


def solution(mesh):
    return jax.shard_map(
        local,
        mesh=mesh,
        in_specs=(
            P("dp", "tensor", None),
            P("dp", "tensor"),
            P(),
            P(),
            P(),
            P(),
            P(),
            P(None, "dp"),
            P(None, "dp"),
            P("dp"),
            P("dp"),
            P("dp", None),
            P(),
            P(None, ("dp", "tensor")),
            P(("dp", "tensor")),
        ),
        out_specs=(P("dp", "tensor", None), P(), P()),
        check_vma=False,
    )
```

profile of v0, /device:TPU:1, one launch (start us, length us, event | category | flops | bytes accessed | tf_op | source)
XLA Modules:
  0.0 689.7 jit_solution(16697699601182889394)
XLA Ops:
  7.2 1.2 fusion.143
  8.5 3.4 fusion.186
  11.9 0.7 slice.147
  13.1 0.7 multiply_convert_fusion.3
  14.2 46.0 %all-gather = s32[1,4096]{1,0:T(1,128)S(1)} all-gather(s32[1,128]{1,0:T(1,128)S(1)} %copy-done.26), channel_id=2, replica_groups=mesh['dp'=8,'tensor'=32] {'tensor'}, dimensions={1}, use_global_device_ids=true | all-gather | bytes 16896 | tf_op jit(solution)/shard_map/all_gather | solution.py:62
  60.5 1.2 fusion.145
  61.7 19.2 %all-gather.8.cloned.1.call-done = bf16[4096,640]{1,0:T(8,128)(2,1)} async-done(((bf16[128,640]{1,0:T(8,128)(2,1)}), bf16[4096,640]{1,0:T(8,128)(2,1)}) %all-gather.8.cloned.1.call-update) | async-done | bytes 5242896 | tf_op jit(solution)/shard_map/all_gather | solution.py:61
  80.8 4.5 fusion.191
  85.3 2.2 copy.88
  87.5 58.2 %all-gather.6.cloned.1.call-done = bf16[4096,640]{1,0:T(8,128)(2,1)} async-done(((bf16[128,640]{1,0:T(8,128)(2,1)}), bf16[4096,640]{1,0:T(8,128)(2,1)}) %all-gather.6.cloned.1.call-update) | async-done | bytes 5242896 | tf_op jit(solution)/shard_map/all_gather | solution.py:60
  145.7 4.9 fusion.192
  150.6 2.2 copy.77
  152.8 2.2 copy.91
  154.9 2.2 copy.89
  157.1 2.2 copy.87
  159.3 2.2 copy.85
  161.5 2.2 copy.83
  163.7 2.2 copy.81
  165.9 2.2 copy.79
  168.1 2.2 copy.92
  170.3 2.2 copy.90
  172.4 2.2 copy.86
  174.6 2.2 copy.84
  176.8 2.2 copy.82
  179.0 1.1 copy.80
  180.1 1.1 copy.78
  181.2 1.8 select_reduce_fusion.6
  183.0 0.7 select_reduce_fusion.5
  184.1 0.7 select_reduce_fusion.4
  184.8 0.7 select_reduce_fusion.3
  185.8 0.7 select_reduce_fusion.2
  186.6 0.7 select_reduce_fusion.1
  187.6 0.7 select_reduce_fusion
  188.4 0.7 select_reduce_fusion.7
  189.4 0.7 fusion.97
  190.2 1.8 fusion.4
  192.0 0.7 fusion.100
  193.1 0.7 fusion.124
  193.9 1.6 fusion.12
  195.5 0.7 fusion.127
  196.6 0.7 fusion.94
  197.3 1.6 fusion
  199.0 0.7 fusion.103
  199.7 1.6 fusion.8
  201.4 0.8 fusion.130
  202.5 0.8 fusion.137
  203.3 0.6 copy-done.11
  203.9 0.5 multiply_reduce_fusion.2
  204.8 1.0 multiply_convert_fusion.2
  206.1 81.0 %all-gather.10.cloned.1.call-done = bf16[1024,1280]{1,0:T(8,128)(2,1)} async-done(((bf16[128,1280]{1,0:T(8,128)(2,1)}), bf16[1024,1280]{1,0:T(8,128)(2,1)}) %all-gather.10.cloned.1.call-update) | async-done | bytes 2621456 | tf_op jit(solution)/shard_map/all_gather | solution.py:106
  287.2 5.9 fusion.194
  293.1 8.4 %convolution_convert_fusion = bf16[1024,1280]{1,0:T(8,128)(2,1)} fusion(bf16[640,1280]{1,0:T(8,128)(2,1)S(1)} %copy-done, f32[1024,640]{1,0:T(8,128)} %fusion.194, bf16[1024,1280]{1,0:T(8,128)(2,1)} %all-gather.10.cloned.1.call-done, bf16[1280,640]{1,0:T(8,128)(2,1)S(1)} %copy-done.27, f32[640]{0:T(1024)S(1)} %copy-done.28, f32[640]{0:T(1024)S(1)} %copy-done.29), kind=kOutput, calls=%fused_computation | convolution fusion | flops 3361996800 | bytes 11146240 | tf_op jit(solution)/shard_map/dot_general | solution.py:111
  301.6 0.6 copy-done.30
  302.2 0.6 dynamic-slice
  304.0 94.9 %reduce-scatter.2.cloned.1.call-done = bf16[128,1280]{1,0:T(8,128)(2,1)} async-done(((bf16[1024,1280]{1,0:T(8,128)(2,1)}), bf16[128,1280]{1,0:T(8,128)(2,1)}) %reduce-scatter.2.cloned.1.call-update) | async-done | bytes 327696 | tf_op jit(solution)/shard_map/reduce_scatter | solution.py:110
  398.9 1.1 fusion.142
  400.1 1.3 multiply_reduce_fusion
  401.4 1.4 multiply_convert_fusion.1
  403.2 130.5 %all-reduce.1 = (bf16[4,1280]{1,0:T(4,128)(2,1)S(1)}, bf16[4]{0:T(256)(128)(2,1)S(1)}, bf16[4,1280]{1,0:T(4,128)(2,1)S(1)}) all-reduce(bf16[4,1280]{1,0:T(4,128)(2,1)S(1)} %convolution_convert_fusion.2, bf16[4]{0:T(256)(128)(2,1)S(1)} %convert_reduce_fusion.1, ...), channel_id=1, replica_groups=mesh['dp'=8,'tensor'=32] {'tensor'}, use_global_device_ids=true, to_apply=%region_24.25 | all-reduce | flops 10244 | bytes 40976 | tf_op jit(solution)/shard_map/psum | solution.py:132
  533.7 37.8 %all-gather.1 = bf16[8,4,1280]{2,1,0:T(4,128)(2,1)S(1)} all-gather(bf16[1,4,1280]{2,1,0:T(4,128)(2,1)S(1)} %bitcast.282), channel_id=1, replica_groups=mesh['dp'=8,'tensor'=32] {'dp'}, dimensions={0}, use_global_device_ids=true | all-gather | bytes 92160 | tf_op jit(solution)/shard_map/all_gather | solution.py:140
  572.1 23.2 %all-reduce = f32[32]{0:T(128)S(1)} all-reduce(f32[32]{0:T(128)S(1)} %sqrt_dynamic-update-slice_fusion), channel_id=1, replica_groups=mesh['dp'=8,'tensor'=32] {'dp'}, use_global_device_ids=true, to_apply=%add | all-reduce | flops 32 | bytes 256
  595.3 86.5 %pmax.7 = f32[32]{0:T(128)S(1)} all-reduce(f32[32]{0:T(128)S(1)} %fusion.133), channel_id=1, replica_groups=mesh['dp'=8,'tensor'=32] {'dp','tensor'}, use_global_device_ids=true, to_apply=%region_33.34 | all-reduce | flops 32 | bytes 256 | tf_op jit(solution)/shard_map/pmax | solution.py:146
  681.8 0.7 convolution_bitcast_fusion.1
  682.5 0.7 convolution_bitcast_fusion
  (116 shorter events, 6.0 us)
Async XLA Ops:
  7.2 285.9 %copy-start = (bf16[640,1280]{1,0:T(8,128)(2,1)S(1)}, bf16[640,1280]{1,0:T(8,128)(2,1)}, u32[]{:S(2)}) copy-start(bf16[640,1280]{1,0:T(8,128)(2,1)} %param.26) | copy-start | bytes 4915204
  7.2 73.7 %all-gather.8.cloned.1.call-start = ((), (), s32[]{:S(2)}) async-start(), calls=%async_computation.2 | async-start | bytes 5406720 | tf_op jit(solution)/shard_map/all_gather | solution.py:61
  11.9 1.2 copy-start.25
  12.6 1.6 copy-start.26
  12.6 133.1 %all-gather.6.cloned.1.call-start = ((), (), s32[]{:S(2)}) async-start(), calls=%async_computation.1 | async-start | bytes 5406720 | tf_op jit(solution)/shard_map/all_gather | solution.py:60
  13.9 273.3 %all-gather.10.cloned.1.call-start = ((), (), s32[]{:S(2)}) async-start(), calls=%async_computation.3 | async-start | bytes 2949120 | tf_op jit(solution)/shard_map/all_gather | solution.py:106
  180.1 2.9 copy-start.10
  181.2 1.8 copy-start.21
  183.0 1.1 copy-start.9
  183.0 1.1 copy-start.20
  183.7 1.1 copy-start.8
  184.7 1.1 copy-start.7
  185.5 1.1 copy-start.6
  186.5 1.1 copy-start.5
  187.3 1.1 copy-start.4
  188.3 1.1 copy-start.19
  190.2 1.8 copy-start.18
  192.0 1.1 copy-start.17
  193.8 1.6 copy-start.15
  195.5 1.1 copy-start.16
  197.3 1.6 copy-start.14
  199.7 1.7 copy-start.13
  201.4 1.1 copy-start.12
  202.5 1.4 copy-start.11
  202.5 2.0 copy-start.23
  203.3 1.2 copy-start.1
  205.8 87.3 %copy-start.27 = (bf16[1280,640]{1,0:T(8,128)(2,1)S(1)}, bf16[1280,640]{1,0:T(8,128)(2,1)}, u32[]{:S(2)}) copy-start(bf16[1280,640]{1,0:T(8,128)(2,1)} %param.23) | copy-start | bytes 4915204
  205.8 87.2 %copy-start.28 = (f32[640]{0:T(1024)S(1)}, f32[640]{0:T(1024)}, u32[]{:S(2)}) copy-start(f32[640]{0:T(1024)} %param.25) | copy-start | bytes 7684
  205.8 87.2 %copy-start.29 = (f32[640]{0:T(1024)S(1)}, f32[640]{0:T(1024)}, u32[]{:S(2)}) copy-start(f32[640]{0:T(1024)} %param.24) | copy-start | bytes 7684
  205.9 193.1 %reduce-scatter.2.cloned.1.call-start = ((), (), s32[]{:S(2)}) async-start(), calls=%async_computation.4 | async-start | bytes 2949120 | tf_op jit(solution)/shard_map/reduce_scatter | solution.py:110
  301.5 0.7 copy-start.30
  301.5 0.7 copy-start.32
  301.5 98.5 %copy-start.2 = (bf16[128,1280]{1,0:T(8,128)(2,1)S(1)}, bf16[128,1280]{1,0:T(8,128)(2,1)}, u32[]{:S(2)}) copy-start(bf16[128,1280]{1,0:T(8,128)(2,1)} %multiply_convert_fusion.2) | copy-start | bytes 983044
  301.5 98.5 %copy-start.24 = (f32[1280]{0:T(1024)S(1)}, f32[1280]{0:T(1024)}, u32[]{:S(2)}) copy-start(f32[1280]{0:T(1024)} %param.27) | copy-start | bytes 15364
  301.5 270.3 %copy-start.22 = (bf16[1280,125]{1,0:T(8,128)(2,1)S(1)}, bf16[1280,125]{1,0:T(8,128)(2,1)}, u32[]{:S(2)}) copy-start(bf16[1280,125]{1,0:T(8,128)(2,1)} %param.28) | copy-start | bytes 960004
  301.5 380.2 %copy-start.31 = (s32[32]{0:T(128)S(1)}, s32[32]{0:T(128)}, u32[]{:S(2)}) copy-start(s32[32]{0:T(128)} %param.17) | copy-start | bytes 388
  402.8 280.4 %copy-start.3 = (bf16[128,1280]{1,0:T(8,128)(2,1)}, bf16[128,1280]{1,0:T(8,128)(2,1)S(1)}, u32[]{:S(2)}) copy-start(bf16[128,1280]{1,0:T(8,128)(2,1)S(1)} %multiply_convert_fusion.1) | copy-start | bytes 983044
Sparse Core Ops, SparseCore 0:
  12.7 68.0 all-gather.7
  82.7 62.9 all-gather.5
  205.9 81.1 all-gather.9
  301.7 97.1 reduce-scatter.1
where the time goes:
time: 691 us; the launch traced here: 690 us
  blocking collectives  324 us (47%)
  waiting for transfers between devices  253 us (37%)
  local copies, waits for them, and re-layouts  47.8 us (7%)
  matrix products  33 us (5%)
  other arithmetic  16.1 us (2%)
  between operations  15 us (2%)
    psum x1, blocking collectives, local(): lax.psum(row_sums.astype(jnp.bfloat16), 'tensor').astype(jnp.float32)  131 us
    reduce_scatter x1, waiting for transfers between devices, local(): lax.psum_scatter(jnp.dot(hidden, w_down, preferred_element_type=jnp.float...  94.9 us
    pmax x1, blocking collectives, local(): every_max = lax.pmax(jnp.max(logits, axis=1), ('dp', 'tensor'))  86.5 us
    all_gather x1, waiting for transfers between devices, local(): received = lax.all_gather(mid_rows, 'dp', axis=0, tiled=True)  81 us
    all_gather x1, waiting for transfers between devices, local(): key_all = lax.all_gather(key_rows, 'tensor', axis=0, tiled=True)  58.2 us
    all_gather x1, blocking collectives, local(): seg_all = lax.all_gather(segments, 'tensor', axis=0, tiled=True)  46 us
    all_gather x1, blocking collectives, local(): lax.all_gather(last_rows, 'dp', axis=0, tiled=True)  37.8 us
    unnamed x1, blocking collectives  23.2 us
  transfers between devices with their start and end apart: 4, of which 4 were waited for; matrix products, arithmetic and copies ran while one was open for 2% of the time, Pallas kernels for 0%

commit v1 on v0

--- a/solution.py
+++ b/solution.py
@@ -137,7 +137,9 @@
     group_norm = jnp.sqrt(jnp.mean(request_mean * request_mean, axis=1))
     slot_count = lax.axis_size("dp") * REQS
     every_last, every_norm = (
-        lax.all_gather(last_rows, "dp", axis=0, tiled=True),
+        jnp.concatenate(
+            lax.all_to_all(jnp.stack([last_rows] * lax.axis_size("dp")), "dp", 0, 0), axis=0
+        ),
         lax.all_gather(group_norm, "dp", axis=0, tiled=True),
     )
     logits = jnp.dot(

time: 691 us -> 657 us (0.951)
  blocking collectives: 324 us -> 285 us
    all_gather x1 -> x0, blocking collectives: 37.8 us -> none  [local(): lax.all_gather(last_rows, 'dp', axis=0, tiled=True)]
  transfers between devices with their start and end apart: 4 -> 5, of which waited for: 4 -> 4; matrix products, arithmetic and copies ran while one was open for 2% -> 2% of each run, Pallas kernels for 0% -> 0%
where the time goes in v1:
time: 657 us; the launch traced here: 656 us
  blocking collectives  285 us (43%)
  waiting for transfers between devices  253 us (39%)
  local copies, waits for them, and re-layouts  48.5 us (7%)
  matrix products  33 us (5%)
  other arithmetic  16.1 us (2%)
  between operations  15 us (2%)
    psum x1, blocking collectives, local(): lax.psum(row_sums.astype(jnp.bfloat16), 'tensor').astype(jnp.float32)  131 us
    reduce_scatter x1, waiting for transfers between devices, local(): lax.psum_scatter(jnp.dot(hidden, w_down, preferred_element_type=jnp.float...  94.9 us
    all_gather x1, waiting for transfers between devices, local(): received = lax.all_gather(mid_rows, 'dp', axis=0, tiled=True)  81 us
    pmax x1, blocking collectives, local(): every_max = lax.pmax(jnp.max(logits, axis=1), ('dp', 'tensor'))  80.7 us
    all_gather x1, waiting for transfers between devices, local(): key_all = lax.all_gather(key_rows, 'tensor', axis=0, tiled=True)  58.2 us
    all_gather x1, blocking collectives, local(): seg_all = lax.all_gather(segments, 'tensor', axis=0, tiled=True)  46 us
    unnamed x1, blocking collectives  28 us
    slice x9, local copies, waits for them, and re-layouts, local(): key_part = key_all[begin:begin + step_size]  22.4 us
  transfers between devices with their start and end apart: 5, of which 4 were waited for; matrix products, arithmetic and copies ran while one was open for 2% of the time, Pallas kernels for 0%

profile of v1, /device:TPU:1, one launch (start us, length us, event | category | flops | bytes accessed | tf_op | source)
XLA Modules:
  0.0 655.7 jit_solution(16564018672586010312)
XLA Ops:
  7.2 1.2 fusion.143
  8.5 3.4 fusion.186
  11.9 0.7 slice.147
  13.1 0.7 multiply_convert_fusion.3
  14.2 46.0 %all-gather = s32[1,4096]{1,0:T(1,128)S(1)} all-gather(s32[1,128]{1,0:T(1,128)S(1)} %copy-done.26), channel_id=2, replica_groups=mesh['dp'=8,'tensor'=32] {'tensor'}, dimensions={1}, use_global_device_ids=true | all-gather | bytes 16896 | tf_op jit(solution)/shard_map/all_gather | solution.py:62
  60.5 1.2 fusion.145
  61.7 19.2 %all-gather.7.cloned.1.call-done = bf16[4096,640]{1,0:T(8,128)(2,1)} async-done(((bf16[128,640]{1,0:T(8,128)(2,1)}), bf16[4096,640]{1,0:T(8,128)(2,1)}) %all-gather.7.cloned.1.call-update) | async-done | bytes 5242896 | tf_op jit(solution)/shard_map/all_gather | solution.py:61
  80.8 4.5 fusion.191
  85.3 2.2 copy.69
  87.5 58.2 %all-gather.5.cloned.1.call-done = bf16[4096,640]{1,0:T(8,128)(2,1)} async-done(((bf16[128,640]{1,0:T(8,128)(2,1)}), bf16[4096,640]{1,0:T(8,128)(2,1)}) %all-gather.5.cloned.1.call-update) | async-done | bytes 5242896 | tf_op jit(solution)/shard_map/all_gather | solution.py:60
  145.7 4.9 fusion.192
  150.6 2.2 copy.58
  152.8 2.2 copy.72
  154.9 2.2 copy.70
  157.1 2.2 copy.68
  159.3 2.2 copy.66
  161.5 2.2 copy.64
  163.7 2.2 copy.62
  165.9 2.2 copy.60
  168.1 2.2 copy.73
  170.3 2.2 copy.71
  172.4 2.2 copy.67
  174.6 2.2 copy.65
  176.8 2.2 copy.63
  179.0 1.1 copy.61
  180.1 1.1 copy.59
  181.2 1.8 select_reduce_fusion.6
  183.0 0.7 select_reduce_fusion.5
  184.1 0.7 select_reduce_fusion.4
  184.8 0.7 select_reduce_fusion.3
  185.8 0.7 select_reduce_fusion.2
  186.6 0.7 select_reduce_fusion.1
  187.6 0.7 select_reduce_fusion
  188.4 0.7 select_reduce_fusion.7
  189.4 0.7 fusion.97
  190.2 1.8 fusion.4
  192.0 0.7 fusion.100
  193.1 0.7 fusion.124
  193.9 1.6 fusion.12
  195.5 0.7 fusion.127
  196.6 0.7 fusion.94
  197.3 1.6 fusion
  199.0 0.7 fusion.103
  199.7 1.6 fusion.8
  201.4 0.8 fusion.130
  202.5 0.8 fusion.137
  203.3 0.6 copy-done.11
  204.8 1.0 multiply_convert_fusion.2
  206.1 81.0 %all-gather.9.cloned.1.call-done = bf16[1024,1280]{1,0:T(8,128)(2,1)} async-done(((bf16[128,1280]{1,0:T(8,128)(2,1)}), bf16[1024,1280]{1,0:T(8,128)(2,1)}) %all-gather.9.cloned.1.call-update) | async-done | bytes 2621456 | tf_op jit(solution)/shard_map/all_gather | solution.py:106
  287.2 5.9 fusion.194
  293.1 8.4 %convolution_convert_fusion = bf16[1024,1280]{1,0:T(8,128)(2,1)} fusion(bf16[640,1280]{1,0:T(8,128)(2,1)S(1)} %copy-done, f32[1024,640]{1,0:T(8,128)} %fusion.194, bf16[1024,1280]{1,0:T(8,128)(2,1)} %all-gather.9.cloned.1.call-done, bf16[1280,640]{1,0:T(8,128)(2,1)S(1)} %copy-done.27, f32[640]{0:T(1024)S(1)} %copy-done.28, f32[640]{0:T(1024)S(1)} %copy-done.29), kind=kOutput, calls=%fused_computation | convolution fusion | flops 3361996800 | bytes 11146240 | tf_op jit(solution)/shard_map/dot_general | solution.py:111
  301.6 0.6 copy-done.30
  302.2 0.6 dynamic-slice
  304.0 94.9 %reduce-scatter.2.cloned.1.call-done = bf16[128,1280]{1,0:T(8,128)(2,1)} async-done(((bf16[1024,1280]{1,0:T(8,128)(2,1)}), bf16[128,1280]{1,0:T(8,128)(2,1)}) %reduce-scatter.2.cloned.1.call-update) | async-done | bytes 327696 | tf_op jit(solution)/shard_map/reduce_scatter | solution.py:110
  398.9 1.1 fusion.142
  400.1 1.3 multiply_reduce_fusion
  401.4 1.4 multiply_convert_fusion.1
  403.2 130.5 %all-reduce.1 = (bf16[4,1280]{1,0:T(4,128)(2,1)S(1)}, bf16[4]{0:T(256)(128)(2,1)S(1)}, bf16[4,1280]{1,0:T(4,128)(2,1)S(1)}) all-reduce(bf16[4,1280]{1,0:T(4,128)(2,1)S(1)} %convolution_convert_fusion.2, bf16[4]{0:T(256)(128)(2,1)S(1)} %convert_reduce_fusion.1, ...), channel_id=1, replica_groups=mesh['dp'=8,'tensor'=32] {'tensor'}, use_global_device_ids=true, to_apply=%region_24.25 | all-reduce | flops 10244 | bytes 40976 | tf_op jit(solution)/shard_map/psum | solution.py:132
  533.7 0.6 stack.2
  534.4 4.1 all-to-all-start
  538.7 28.0 %all-reduce = f32[32]{0:T(128)S(1)} all-reduce(f32[32]{0:T(128)S(1)} %sqrt_dynamic-update-slice_fusion), channel_id=1, replica_groups=mesh['dp'=8,'tensor'=32] {'dp'}, use_global_device_ids=true, to_apply=%add | all-reduce | flops 32 | bytes 256
  567.0 0.7 convolution_bitcast_fusion.1
  567.7 80.7 %pmax.7 = f32[32]{0:T(128)S(1)} all-reduce(f32[32]{0:T(128)S(1)} %fusion.133), channel_id=1, replica_groups=mesh['dp'=8,'tensor'=32] {'dp','tensor'}, use_global_device_ids=true, to_apply=%region_33.34 | all-reduce | flops 32 | bytes 256 | tf_op jit(solution)/shard_map/pmax | solution.py:148
  648.5 0.7 convolution_bitcast_fusion
  (118 shorter events, 6.5 us)
Async XLA Ops:
  7.2 285.9 %copy-start = (bf16[640,1280]{1,0:T(8,128)(2,1)S(1)}, bf16[640,1280]{1,0:T(8,128)(2,1)}, u32[]{:S(2)}) copy-start(bf16[640,1280]{1,0:T(8,128)(2,1)} %param.26) | copy-start | bytes 4915204
  7.2 73.7 %all-gather.7.cloned.1.call-start = ((), (), s32[]{:S(2)}) async-start(), calls=%async_computation.3 | async-start | bytes 5406720 | tf_op jit(solution)/shard_map/all_gather | solution.py:61
  11.9 1.2 copy-start.25
  12.6 1.6 copy-start.26
  12.6 133.1 %all-gather.5.cloned.1.call-start = ((), (), s32[]{:S(2)}) async-start(), calls=%async_computation.2 | async-start | bytes 5406720 | tf_op jit(solution)/shard_map/all_gather | solution.py:60
  13.9 273.3 %all-gather.9.cloned.1.call-start = ((), (), s32[]{:S(2)}) async-start(), calls=%async_computation.4 | async-start | bytes 2949120 | tf_op jit(solution)/shard_map/all_gather | solution.py:106
  180.1 2.9 copy-start.10
  181.2 1.8 copy-start.21
  183.0 1.1 copy-start.9
  183.0 1.1 copy-start.20
  183.7 1.1 copy-start.8
  184.7 1.1 copy-start.7
  185.5 1.1 copy-start.6
  186.5 1.1 copy-start.5
  187.3 1.1 copy-start.4
  188.3 1.1 copy-start.19
  190.2 1.8 copy-start.18
  192.0 1.1 copy-start.17
  193.8 1.6 copy-start.15
  195.5 1.1 copy-start.16
  197.3 1.6 copy-start.14
  199.7 1.7 copy-start.13
  201.4 1.1 copy-start.12
  202.5 1.4 copy-start.11
  202.5 2.0 copy-start.23
  203.3 1.2 copy-start.1
  205.8 87.3 %copy-start.27 = (bf16[1280,640]{1,0:T(8,128)(2,1)S(1)}, bf16[1280,640]{1,0:T(8,128)(2,1)}, u32[]{:S(2)}) copy-start(bf16[1280,640]{1,0:T(8,128)(2,1)} %param.23) | copy-start | bytes 4915204
  205.8 87.2 %copy-start.28 = (f32[640]{0:T(1024)S(1)}, f32[640]{0:T(1024)}, u32[]{:S(2)}) copy-start(f32[640]{0:T(1024)} %param.25) | copy-start | bytes 7684
  205.8 87.2 %copy-start.29 = (f32[640]{0:T(1024)S(1)}, f32[640]{0:T(1024)}, u32[]{:S(2)}) copy-start(f32[640]{0:T(1024)} %param.24) | copy-start | bytes 7684
  205.9 193.1 %reduce-scatter.2.cloned.1.call-start = ((), (), s32[]{:S(2)}) async-start(), calls=%async_computation.5 | async-start | bytes 2949120 | tf_op jit(solution)/shard_map/reduce_scatter | solution.py:110
  301.5 0.7 copy-start.30
  301.5 0.7 copy-start.32
  301.5 98.5 %copy-start.2 = (bf16[128,1280]{1,0:T(8,128)(2,1)S(1)}, bf16[128,1280]{1,0:T(8,128)(2,1)}, u32[]{:S(2)}) copy-start(bf16[128,1280]{1,0:T(8,128)(2,1)} %multiply_convert_fusion.2) | copy-start | bytes 983044
  301.5 98.5 %copy-start.24 = (f32[1280]{0:T(1024)S(1)}, f32[1280]{0:T(1024)}, u32[]{:S(2)}) copy-start(f32[1280]{0:T(1024)} %param.27) | copy-start | bytes 15364
  301.5 265.2 %copy-start.22 = (bf16[1280,125]{1,0:T(8,128)(2,1)S(1)}, bf16[1280,125]{1,0:T(8,128)(2,1)}, u32[]{:S(2)}) copy-start(bf16[1280,125]{1,0:T(8,128)(2,1)} %param.28) | copy-start | bytes 960004
  301.5 265.5 %copy-start.31 = (s32[32]{0:T(128)S(1)}, s32[32]{0:T(128)}, u32[]{:S(2)}) copy-start(s32[32]{0:T(128)} %param.17) | copy-start | bytes 388
  402.8 246.4 %copy-start.3 = (bf16[128,1280]{1,0:T(8,128)(2,1)}, bf16[128,1280]{1,0:T(8,128)(2,1)S(1)}, u32[]{:S(2)}) copy-start(bf16[128,1280]{1,0:T(8,128)(2,1)S(1)} %multiply_convert_fusion.1) | copy-start | bytes 983044
  534.4 32.3 %all-to-all-start = ((bf16[8,4,1280]{2,1,0:T(4,128)(2,1)}), bf16[8,4,1280]{2,1,0:T(4,128)(2,1)S(1)}, u32[]{:S(2)}, u32[]{:S(2)}) async-start(bf16[8,4,1280]{2,1,0:T(4,128)(2,1)} %stack.2), calls=%async_computation.1 | async-start | bytes 163840 | tf_op jit(solution)/shard_map/all_to_all | solution.py:141
Sparse Core Ops, SparseCore 0:
  12.7 68.0 all-gather.6
  82.7 62.9 all-gather.4
  205.9 81.1 all-gather.8
  301.7 97.1 reduce-scatter.1
